TPU v7x, 256 devices: a whole 4x4x8 slice. The times are simulated.
256 devices in a mesh: gx: 16 (over x, z_hi, core), gy: 4 (over z_lo), gz: 4 (over y).
Axes of the slice: x: 4, y: 4, z: 8 (z_hi: 2, z_lo: 4; z = z_hi * 4 + z_lo), core: 2. Of those that a mesh axis runs over, the one named last changes fastest.
Arguments:
- image_slab: float32 [64, 1024, 1024], P(('gz', 'gx'), None, 'gy'), may hold values from -6 to 6
- deformed_slab: float32 [64, 1024, 1024], P(('gz', 'gx'), None, 'gy'), may hold values from -6 to 6
- shifts: int32 [2, 3, 4, 16, 4], P(None, None, 'gz', 'gx', 'gy'), may hold values from -8 to 8, as said below
Outputs:
- displacement: float32 [3, 12, 144, 132], P(None, 'gz', 'gx', 'gy')
- residual_map: float32 [64, 1024, 1024], P('gz', 'gx', 'gy')
Inputs may be any that keep to these rules, and one draw needn't show every extreme that they name: `shifts`: every component lies within -8 to 8, and both ends are taken by some entry.
All inputs are finite; a program needn't handle non-finite values.
Results may differ from a plain program's by a relative error of at most 0.0003.
Values sent between devices are 32-bit elements; how exact they have to be, the bound alone decides.
No kernel may reach another device: no remote copies, remote signals or barrier semaphores. Data moves between devices by JAX's collectives and lax.ppermute only.
A program may use at most 128 MiB of HBM per device.

v0:
```python
import numpy as np
import jax
import jax.numpy as jnp
from jax import lax
from jax.sharding import PartitionSpec as P

ELEMENT = 8
DMAX = 8
ITERS = 2
SWEEPS = 3
DAMPING = 0.7
REGULARIZE = 4.0
HI = lax.Precision.HIGHEST


def shape_table(voxel_count, squared=False):
    voxel = np.arange(voxel_count)
    fraction = ((voxel % ELEMENT).astype(np.float32) + 0.5) / ELEMENT
    owning = voxel // ELEMENT
    nodes = np.arange(voxel_count // ELEMENT + 1)
    lower = (nodes[None, :] == owning[:, None]) * (1.0 - fraction)[:, None]
    upper = (nodes[None, :] == owning[:, None] + 1) * fraction[:, None]
    table = (lower + upper).astype(np.float32)
    if squared:
        table = table * table
    return jnp.asarray(table)


def z_weights(squared=False):
    fraction = (np.arange(ELEMENT, dtype=np.float32) + 0.5) / ELEMENT
    lower = 1.0 - fraction
    if squared:
        return (lower * lower, fraction * fraction)
    return (lower, fraction)


def neighbours(axis):
    count = lax.axis_size(axis)
    forward = [(i, i + 1) for i in range(count - 1)]
    backward = [(i + 1, i) for i in range(count - 1)]
    return (forward, backward)


def halo(block, axis, dim, width):
    forward, backward = neighbours(axis)
    size = block.shape[dim]
    low = lax.ppermute(lax.slice_in_dim(block, size - width, size, axis=dim), axis, forward)
    high = lax.ppermute(lax.slice_in_dim(block, 0, width, axis=dim), axis, backward)
    return jnp.concatenate([low, block, high], axis=dim)


def share(partial_value):
    value = partial_value
    for axis, dim in (("gz", 1), ("gx", 2), ("gy", 3)):
        forward, backward = neighbours(axis)
        size = value.shape[dim]
        first = lax.slice_in_dim(value, 0, 1, axis=dim)
        last = lax.slice_in_dim(value, size - 1, size, axis=dim)
        from_low = lax.ppermute(last, axis, forward)
        from_high = lax.ppermute(first, axis, backward)
        middle = lax.slice_in_dim(value, 1, size - 1, axis=dim)
        value = jnp.concatenate([first + from_low, middle, last + from_high], axis=dim)
    return value


def cut_range(array, axis, start, length):
    return lax.slice_in_dim(array, start, start + length, axis=axis)


def smooth(array, axis):
    length = array.shape[axis] - 2
    return (
        cut_range(array, axis, 0, length)
        + 2.0 * cut_range(array, axis, 1, length)
        + cut_range(array, axis, 2, length)
    ) * 0.25


def differ(array, axis):
    length = array.shape[axis] - 2
    return (cut_range(array, axis, 2, length) - cut_range(array, axis, 0, length)) * 0.5


def gradients(extended):
    along_z = smooth(smooth(differ(extended, 0), 1), 2)
    along_x = smooth(smooth(differ(extended, 1), 0), 2)
    along_y = smooth(smooth(differ(extended, 2), 0), 1)
    return jnp.stack([along_z, along_x, along_y])


def interp_xy(nodal, table_x, table_y):
    step = jnp.einsum("cabd,yd->caby", nodal, table_y, precision=HI)
    return jnp.einsum("caby,xb->caxy", step, table_x, precision=HI)


def expand_z(values, weights):
    lower, upper = weights
    count = values.shape[1] - 1
    low = values[:, :count, None]
    high = values[:, 1:, None]
    shape = (1, 1, ELEMENT, 1, 1)
    joined = low * lower.reshape(shape) + high * upper.reshape(shape)
    return joined.reshape((values.shape[0], count * ELEMENT) + values.shape[2:])


def interpolate(nodal, tables, weights):
    return expand_z(interp_xy(nodal, *tables), weights)


def reduce_z(field, weights):
    lower, upper = weights
    count = field.shape[1] // ELEMENT
    blocks = field.reshape((field.shape[0], count, ELEMENT) + field.shape[2:])
    shape = (1, 1, ELEMENT, 1, 1)
    low = jnp.sum(blocks * lower.reshape(shape), axis=2)
    high = jnp.sum(blocks * upper.reshape(shape), axis=2)
    parts = [low[:, :1]]
    for e in range(1, count):
        parts.append(high[:, e - 1 : e] + low[:, e : e + 1])
    parts.append(high[:, count - 1 :])
    return jnp.concatenate(parts, axis=1)


def restrict(field, tables, weights):
    table_x, table_y = tables
    step = reduce_z(field, weights)
    step = jnp.einsum("caxy,xb->caby", step, table_x, precision=HI)
    return jnp.einsum("caby,yd->cabd", step, table_y, precision=HI)


def invert(diag):
    a, b, c, d, e, f = (diag[0], diag[1], diag[2], diag[3], diag[4], diag[5])
    i00 = b * c - f * f
    i11 = a * c - e * e
    i22 = a * b - d * d
    i01 = e * f - d * c
    i02 = d * f - b * e
    i12 = d * e - a * f
    det = a * i00 + d * i01 + e * i02
    return jnp.stack([i00, i11, i22, i01, i02, i12]) / det


def apply_inverse(inverse, vector):
    out_z = inverse[0] * vector[0] + inverse[3] * vector[1] + inverse[4] * vector[2]
    out_x = inverse[3] * vector[0] + inverse[1] * vector[1] + inverse[5] * vector[2]
    out_y = inverse[4] * vector[0] + inverse[5] * vector[1] + inverse[2] * vector[2]
    return jnp.stack([out_z, out_x, out_y])


def bricks_of(image_slab, deformed_slab):
    image = lax.all_to_all(image_slab, "gx", split_axis=1, concat_axis=0, tiled=True)
    deformed = lax.all_to_all(deformed_slab, "gx", split_axis=1, concat_axis=0, tiled=True)
    both = jnp.stack([image, deformed])
    both = halo(both, "gy", 3, DMAX)
    both = halo(both, "gx", 2, DMAX)
    forward, backward = neighbours("gz")
    bz, nx, ny = both.shape[1:]
    image = both[0]
    deformed = both[1]
    to_high = jnp.concatenate([deformed[bz - DMAX :], image[bz - 1 :]], axis=0)
    to_low = jnp.concatenate([deformed[:DMAX], image[:1]], axis=0)
    from_low = lax.ppermute(to_high, "gz", forward)
    from_high = lax.ppermute(to_low, "gz", backward)
    deformed_ext = jnp.concatenate([from_low[:DMAX], deformed, from_high[:DMAX]], axis=0)
    image_ext = jnp.concatenate([from_low[DMAX:], image, from_high[DMAX:]], axis=0)
    image_ext = image_ext[:, DMAX - 1 : nx - DMAX + 1, DMAX - 1 : ny - DMAX + 1]
    return (image_ext, deformed_ext)


def shards(image_slab, deformed_slab, shifts):
    image_ext, deformed_ext = bricks_of(image_slab, deformed_slab)
    image = image_ext[1:-1, 1:-1, 1:-1]
    z_count, x_count, y_count = image.shape
    grads = gradients(image_ext)
    tables = (shape_table(x_count), shape_table(y_count))
    tables_sq = (shape_table(x_count, True), shape_table(y_count, True))
    weights = z_weights(False)
    weights_sq = z_weights(True)
    pairs = ((0, 0), (1, 1), (2, 2), (0, 1), (0, 2), (1, 2))

    def residual(moved, warped_now, offset):
        offset_float = offset.astype(jnp.float32)[:, None, None, None]
        return image - warped_now - jnp.sum(grads * (moved - offset_float), axis=0)

    def warp(iteration):
        offset = shifts[iteration, :, 0, 0, 0]
        starts = [DMAX + offset[0], DMAX + offset[1], DMAX + offset[2]]
        return (lax.dynamic_slice(deformed_ext, starts, (z_count, x_count, y_count)), offset)

    def operator(delta):
        inner = jnp.sum(grads * interpolate(delta, tables, weights), axis=0)
        return share(restrict(grads * inner[None], tables, weights))

    warped, offset = warp(0)
    resid = (
        image - warped + jnp.sum(grads * offset.astype(jnp.float32)[:, None, None, None], axis=0)
    )
    products = jnp.stack([grads[i] * grads[j] for i, j in pairs])
    first = jnp.concatenate(
        [restrict(products, tables_sq, weights_sq), restrict(grads * resid[None], tables, weights)],
        axis=0,
    )
    first = share(first)
    diag = (
        first[:6]
        + REGULARIZE * jnp.array([1.0, 1.0, 1.0, 0.0, 0.0, 0.0], jnp.float32)[:, None, None, None]
    )
    inverse = invert(diag)
    rhs = first[6:]
    nodal = jnp.zeros(
        (3, z_count // ELEMENT + 1, x_count // ELEMENT + 1, y_count // ELEMENT + 1), jnp.float32
    )
    for iteration in range(ITERS):
        if iteration > 0:
            warped, offset = warp(iteration)
            resid = residual(interpolate(nodal, tables, weights), warped, offset)
            rhs = share(restrict(grads * resid[None], tables, weights))
        delta = DAMPING * apply_inverse(inverse, rhs)
        for sweep in range(SWEEPS - 1):
            applied = operator(delta) + REGULARIZE * delta
            delta = delta + DAMPING * apply_inverse(inverse, rhs - applied)
        nodal = nodal + delta
    final = residual(interpolate(nodal, tables, weights), warped, offset)
    return (nodal, final)


def solution(mesh):
    return jax.shard_map(
        shards,
        mesh=mesh,
        in_specs=(
            P(("gz", "gx"), None, "gy"),
            P(("gz", "gx"), None, "gy"),
            P(None, None, "gz", "gx", "gy"),
        ),
        out_specs=(P(None, "gz", "gx", "gy"), P("gz", "gx", "gy")),
        check_vma=False,
    )
```

profile of v0, /device:TPU:4, one launch (start us, length us, event | category | flops | bytes accessed | tf_op | source)
XLA Modules:
  0.0 536.1 jit_solution(17858841931184547508)
XLA Ops:
  0.6 3.4 copy.56
  4.0 11.4 %all-to-all-start.1 = ((f32[1,1024,256]{2,0,1:T(1,128)}), f32[1,1024,256]{2,0,1:T(1,128)S(1)}, u32[]{:S(2)}, u32[]{:S(2)}) async-start(f32[1,1024,256]{2,0,1:T(1,128)} %copy.56), calls=%async_computation.1 | async-start | bytes 2097152 | tf_op jit(solution)/shard_map/all_to_all | solution.py:152
  17.5 18.0 %all-to-all-done.1 = f32[1,1024,256]{2,0,1:T(1,128)S(1)} async-done(((f32[1,1024,256]{2,0,1:T(1,128)}), f32[1,1024,256]{2,0,1:T(1,128)S(1)}, u32[]{:S(2)}, u32[]{:S(2)}) %all-to-all-start.1) | async-done | bytes 1048608 | tf_op jit(solution)/shard_map/all_to_all | solution.py:152
  35.6 6.8 %all-to-all-start = ((f32[1,1024,256]{2,0,1:T(1,128)}), f32[1,1024,256]{2,0,1:T(1,128)}, u32[]{:S(2)}, u32[]{:S(2)}) async-start(f32[1,1024,256]{2,0,1:T(1,128)} %copy.55), calls=%async_computation | async-start | bytes 2097152 | tf_op jit(solution)/shard_map/all_to_all | solution.py:151
  43.3 17.1 %all-to-all-done = f32[1,1024,256]{2,0,1:T(1,128)} async-done(((f32[1,1024,256]{2,0,1:T(1,128)}), f32[1,1024,256]{2,0,1:T(1,128)}, u32[]{:S(2)}, u32[]{:S(2)}) %all-to-all-start) | async-done | bytes 1048608 | tf_op jit(solution)/shard_map/all_to_all | solution.py:151
  60.4 3.9 copy.57
  66.7 15.6 %collective-permute-start = (f32[2,16,64,8]{2,3,1,0:T(8,128)S(1)}, f32[2,16,64,8]{2,3,1,0:T(8,128)S(1)}, u32[]{:S(2)}, u32[]{:S(2)}) collective-permute-start(f32[2,16,64,8]{2,3,1,0:T(8,128)S(1)} %get-tuple-element.59), channel_id=1, source_target_pairs={{0,4},{4,8},{8,12},{1,5},{5,9},{9,13},{2,6},{6,10},{10,14},{3,7},{... | collective-permute-start | bytes 196616 | tf_op jit(solution)/shard_map/ppermute | solution.py:47
  85.6 5.0 fusion.117
  90.6 3.3 copy.60
  95.8 4.0 copy.59
  105.1 13.0 %collective-permute-done.2 = f32[2,16,8,272]{3,2,1,0:T(8,128)} collective-permute-done((f32[2,16,8,272]{3,2,1,0:T(8,128)}, f32[2,16,8,272]{3,2,1,0:T(8,128)}, u32[]{:S(2)}, u32[]{:S(2)}) %collective-permute-start.2) | collective-permute-done | bytes 278560 | tf_op jit(solution)/shard_map/ppermute | solution.py:47
  118.0 3.8 copy.61
  121.8 6.1 %pad_maximum_fusion.2 = f32[2,16,80,272]{2,3,1,0:T(8,128)S(1)} fusion(f32[2,16,8,272]{2,3,1,0:T(8,128)} %copy.62, f32[2,16,64,8]{2,3,1,0:T(8,128)S(1)} %collective-permute-done.1, f32[1,16,64,256]{2,3,1,0:T(8,128)S(1)} %copy.58, f32[1,16,64,256]{2,3,1,0:T(8,128)} %copy.57, f32[2,16,64,8]{2,3,1,0:T(8,128)S(1)} %collective-permute-done, f32[2,16,8,272]{2,3,1,0:T(8,128)} %copy.61), kind=kLoop, calls=%fused_computation.24 | loop fusion | flops 3481600 | bytes 5570560 | tf_op jit(solution)/shard_map/concatenate | solution.py:49
  135.7 4.8 collective-permute-start.5
  145.5 4.7 slice_bitcast_fusion
  150.2 9.6 %collective-permute-done.4 = f32[9,80,272]{2,1,0:T(8,128)} collective-permute-done((f32[9,80,272]{2,1,0:T(8,128)}, f32[9,80,272]{2,1,0:T(8,128)}, u32[]{:S(2)}, u32[]{:S(2)}) %collective-permute-start.4) | collective-permute-done | bytes 783392 | tf_op jit(solution)/shard_map/ppermute | solution.py:163
  182.3 7.9 %multiply_reduce_fusion.1 = (f32[6,2,64,256]{2,3,1,0:T(8,128)S(1)}, f32[6,2,64,256]{2,3,1,0:T(8,128)S(1)}) fusion(f32[6,2,8,64,256]{3,4,2,1,0:T(8,128)} %constant_dynamic-update-slice_fusion, f32[8]{0:T(128)S(1)} %copy-done.74, f32[8]{0:T(128)S(1)} %copy-done.75), kind=kLoop, calls=%fused_computation.1 | loop fusion | flops 5898240 | bytes 7864384 | tf_op jit(solution)/shard_map/reduce_sum | solution.py:115
  226.9 4.4 collective-permute-start.6
  234.6 5.3 collective-permute-done.7
  241.9 8.4 %collective-permute-start.9 = (f32[9,3,1,33]{3,2,1,0:T(1,128)S(1)}, f32[9,3,1,33]{3,2,1,0:T(1,128)S(1)}, u32[]{:S(2)}, u32[]{:S(2)}) collective-permute-start(f32[9,3,1,33]{3,2,1,0:T(1,128)S(1)} %get-tuple-element.126), channel_id=1, source_target_pairs={{16,0},{32,16},{48,32},{64,48},{80,64},{96,80},{112,96},{128,112},... | collective-permute-start | bytes 10700 | tf_op jit(solution)/shard_map/ppermute | solution.py:60
  252.0 4.6 collective-permute-start.10
  260.8 4.7 collective-permute-done.11
  271.2 3.8 multiply_reduce_fusion.17
  275.2 2.9 multiply_reduce_fusion.16
  288.9 3.9 collective-permute-start.12
  294.4 4.4 collective-permute-done.13
  300.8 7.8 %collective-permute-done.14 = f32[3,3,1,33]{3,2,1,0:T(1,128)S(1)} collective-permute-done((f32[3,3,1,33]{3,2,1,0:T(1,128)S(1)}, f32[3,3,1,33]{3,2,1,0:T(1,128)S(1)}, u32[]{:S(2)}, u32[]{:S(2)}) %collective-permute-start.14) | collective-permute-done | bytes 1220 | tf_op jit(solution)/shard_map/ppermute | solution.py:59
  311.9 3.8 collective-permute-start.16
  317.6 4.3 collective-permute-done.17
  327.0 3.7 multiply_reduce_fusion.14
  341.1 3.6 collective-permute-start.18
  346.3 4.2 collective-permute-done.19
  352.4 7.8 %collective-permute-done.20 = f32[3,3,1,33]{3,2,1,0:T(1,128)S(1)} collective-permute-done((f32[3,3,1,33]{3,2,1,0:T(1,128)S(1)}, f32[3,3,1,33]{3,2,1,0:T(1,128)S(1)}, u32[]{:S(2)}, u32[]{:S(2)}) %collective-permute-start.20) | collective-permute-done | bytes 1220 | tf_op jit(solution)/shard_map/ppermute | solution.py:59
  369.9 4.1 collective-permute-done.23
  378.9 3.8 multiply_reduce_fusion.11
  382.7 3.1 bitcast_subtract_fusion.1
  399.5 4.2 collective-permute-done.25
  405.7 7.8 %collective-permute-done.26 = f32[3,3,1,33]{3,2,1,0:T(1,128)S(1)} collective-permute-done((f32[3,3,1,33]{3,2,1,0:T(1,128)S(1)}, f32[3,3,1,33]{3,2,1,0:T(1,128)S(1)}, u32[]{:S(2)}, u32[]{:S(2)}) %collective-permute-start.26) | collective-permute-done | bytes 1220 | tf_op jit(solution)/shard_map/ppermute | solution.py:59
  421.0 4.3 collective-permute-done.29
  429.8 3.7 multiply_reduce_fusion.8
  447.3 4.2 collective-permute-done.31
  453.5 7.8 %collective-permute-done.32 = f32[3,3,1,33]{3,2,1,0:T(1,128)S(1)} collective-permute-done((f32[3,3,1,33]{3,2,1,0:T(1,128)S(1)}, f32[3,3,1,33]{3,2,1,0:T(1,128)S(1)}, u32[]{:S(2)}, u32[]{:S(2)}) %collective-permute-start.32) | collective-permute-done | bytes 1220 | tf_op jit(solution)/shard_map/ppermute | solution.py:59
  468.6 4.3 collective-permute-done.35
  477.4 3.7 multiply_reduce_fusion.5
  494.9 4.2 collective-permute-done.37
  501.1 7.8 %collective-permute-done.38 = f32[3,3,1,33]{3,2,1,0:T(1,128)S(1)} collective-permute-done((f32[3,3,1,33]{3,2,1,0:T(1,128)S(1)}, f32[3,3,1,33]{3,2,1,0:T(1,128)S(1)}, u32[]{:S(2)}, u32[]{:S(2)}) %collective-permute-start.38) | collective-permute-done | bytes 1220 | tf_op jit(solution)/shard_map/ppermute | solution.py:59
  516.2 4.3 collective-permute-done.41
  527.4 3.8 multiply_reduce_fusion.2
  (431 shorter events, 238.3 us)
Async XLA Ops:
  4.0 31.6 %all-to-all-start.1 = ((f32[1,1024,256]{2,0,1:T(1,128)}), f32[1,1024,256]{2,0,1:T(1,128)S(1)}, u32[]{:S(2)}, u32[]{:S(2)}) async-start(f32[1,1024,256]{2,0,1:T(1,128)} %copy.56), calls=%async_computation.1 | async-start | bytes 2097152 | tf_op jit(solution)/shard_map/all_to_all | solution.py:152
  35.6 24.8 %all-to-all-start = ((f32[1,1024,256]{2,0,1:T(1,128)}), f32[1,1024,256]{2,0,1:T(1,128)}, u32[]{:S(2)}, u32[]{:S(2)}) async-start(f32[1,1024,256]{2,0,1:T(1,128)} %copy.55), calls=%async_computation | async-start | bytes 2097152 | tf_op jit(solution)/shard_map/all_to_all | solution.py:151
  65.4 18.7 %collective-permute-start.1 = (f32[2,16,64,8]{2,3,1,0:T(8,128)S(1)}, f32[2,16,64,8]{2,3,1,0:T(8,128)S(1)}, u32[]{:S(2)}, u32[]{:S(2)}) collective-permute-start(f32[2,16,64,8]{2,3,1,0:T(8,128)S(1)} %get-tuple-element.60), channel_id=1, source_target_pairs={{4,0},{8,4},{12,8},{5,1},{9,5},{13,9},{6,2},{10,6},{14,10},{7,3},{... | collective-permute-start | bytes 196616 | tf_op jit(solution)/shard_map/ppermute | solution.py:48
  66.7 18.6 %collective-permute-start = (f32[2,16,64,8]{2,3,1,0:T(8,128)S(1)}, f32[2,16,64,8]{2,3,1,0:T(8,128)S(1)}, u32[]{:S(2)}, u32[]{:S(2)}) collective-permute-start(f32[2,16,64,8]{2,3,1,0:T(8,128)S(1)} %get-tuple-element.59), channel_id=1, source_target_pairs={{0,4},{4,8},{8,12},{1,5},{5,9},{9,13},{2,6},{6,10},{10,14},{3,7},{... | collective-permute-start | bytes 196616 | tf_op jit(solution)/shard_map/ppermute | solution.py:47
  84.0 37.8 %copy-start.26 = (f32[2,16,64,8]{2,3,1,0:T(8,128)}, f32[2,16,64,8]{2,3,1,0:T(8,128)S(1)}, u32[]{:S(2)}) copy-start(f32[2,16,64,8]{2,3,1,0:T(8,128)S(1)} %collective-permute-done.1) | copy-start | bytes 196612
  93.9 8.3 %collective-permute-start.3 = (f32[2,16,8,272]{3,2,1,0:T(8,128)S(1)}, f32[2,16,8,272]{3,2,1,0:T(8,128)S(1)}, u32[]{:S(2)}, u32[]{:S(2)}) collective-permute-start(f32[2,16,8,272]{3,2,1,0:T(8,128)S(1)} %copy.60), channel_id=1, source_target_pairs={{16,0},{32,16},{48,32},{64,48},{80,64},{96,80},{112,96},{128,112},... | collective-permute-start | bytes 835592 | tf_op jit(solution)/shard_map/ppermute | solution.py:48
  99.8 18.2 %collective-permute-start.2 = (f32[2,16,8,272]{3,2,1,0:T(8,128)}, f32[2,16,8,272]{3,2,1,0:T(8,128)}, u32[]{:S(2)}, u32[]{:S(2)}) collective-permute-start(f32[2,16,8,272]{3,2,1,0:T(8,128)} %copy.59), channel_id=1, source_target_pairs={{0,16},{16,32},{32,48},{48,64},{64,80},{80,96},{96,112},{112,128},... | collective-permute-start | bytes 835592 | tf_op jit(solution)/shard_map/ppermute | solution.py:47
  133.7 26.0 %collective-permute-start.4 = (f32[9,80,272]{2,1,0:T(8,128)}, f32[9,80,272]{2,1,0:T(8,128)}, u32[]{:S(2)}, u32[]{:S(2)}) collective-permute-start(f32[9,80,272]{2,1,0:T(8,128)} %copy.63), channel_id=1, source_target_pairs={{1,0},{2,1},{3,2},{5,4},{6,5},{7,6},{9,8},{10,9},{11,10},{13,12},{... | collective-permute-start | bytes 2350088 | tf_op jit(solution)/shard_map/ppermute | solution.py:163
  135.7 25.6 %collective-permute-start.5 = (f32[9,80,272]{2,1,0:T(8,128)S(1)}, f32[9,80,272]{2,1,0:T(8,128)S(1)}, u32[]{:S(2)}, u32[]{:S(2)}) collective-permute-start(f32[9,80,272]{2,1,0:T(8,128)S(1)} %copy.65), channel_id=1, source_target_pairs={{0,1},{1,2},{2,3},{4,5},{5,6},{6,7},{8,9},{9,10},{10,11},{12,13},{... | collective-permute-start | bytes 2350088 | tf_op jit(solution)/shard_map/ppermute | solution.py:162
  226.9 6.4 %collective-permute-start.6 = (f32[9,1,9,33]{3,2,1,0:T(8,128)S(1)}, f32[9,1,9,33]{3,2,1,0:T(8,128)S(1)}, u32[]{:S(2)}, u32[]{:S(2)}) collective-permute-start(f32[9,1,9,33]{3,2,1,0:T(8,128)S(1)} %fusion.60), channel_id=1, source_target_pairs={{0,1},{1,2},{2,3},{4,5},{5,6},{6,7},{8,9},{9,10},{10,11},{12,13},{... | collective-permute-start | bytes 32084 | tf_op jit(solution)/shard_map/ppermute | solution.py:59
  233.3 6.6 %collective-permute-start.7 = (f32[9,1,9,33]{3,2,1,0:T(8,128)S(1)}, f32[9,1,9,33]{3,2,1,0:T(8,128)S(1)}, u32[]{:S(2)}, u32[]{:S(2)}) collective-permute-start(f32[9,1,9,33]{3,2,1,0:T(8,128)S(1)} %get-tuple-element.42), channel_id=1, source_target_pairs={{1,0},{2,1},{3,2},{5,4},{6,5},{7,6},{9,8},{10,9},{11,10},{13,12},{... | collective-permute-start | bytes 32084 | tf_op jit(solution)/shard_map/ppermute | solution.py:60
  240.0 10.4 %collective-permute-start.8 = (f32[9,3,1,33]{3,2,1,0:T(1,128)S(1)}, f32[9,3,1,33]{3,2,1,0:T(1,128)S(1)}, u32[]{:S(2)}, u32[]{:S(2)}) collective-permute-start(f32[9,3,1,33]{3,2,1,0:T(1,128)S(1)} %get-tuple-element.125), channel_id=1, source_target_pairs={{0,16},{16,32},{32,48},{48,64},{64,80},{80,96},{96,112},{112,128},... | collective-permute-start | bytes 10700 | tf_op jit(solution)/shard_map/ppermute | solution.py:59
  241.9 9.9 %collective-permute-start.9 = (f32[9,3,1,33]{3,2,1,0:T(1,128)S(1)}, f32[9,3,1,33]{3,2,1,0:T(1,128)S(1)}, u32[]{:S(2)}, u32[]{:S(2)}) collective-permute-start(f32[9,3,1,33]{3,2,1,0:T(1,128)S(1)} %get-tuple-element.126), channel_id=1, source_target_pairs={{16,0},{32,16},{48,32},{64,48},{80,64},{96,80},{112,96},{128,112},... | collective-permute-start | bytes 10700 | tf_op jit(solution)/shard_map/ppermute | solution.py:60
  252.0 8.8 %collective-permute-start.10 = (f32[9,3,9,1]{3,2,1,0:T(8,128)S(1)}, f32[9,3,9,1]{3,2,1,0:T(8,128)S(1)}, u32[]{:S(2)}, u32[]{:S(2)}) collective-permute-start(f32[9,3,9,1]{3,2,1,0:T(8,128)S(1)} %get-tuple-element.121), channel_id=1, source_target_pairs={{0,4},{4,8},{8,12},{1,5},{5,9},{9,13},{2,6},{6,10},{10,14},{3,7},{... | collective-permute-start | bytes 2924 | tf_op jit(solution)/shard_map/ppermute | solution.py:59
  256.6 8.8 %collective-permute-start.11 = (f32[9,3,9,1]{3,2,1,0:T(8,128)S(1)}, f32[9,3,9,1]{3,2,1,0:T(8,128)S(1)}, u32[]{:S(2)}, u32[]{:S(2)}) collective-permute-start(f32[9,3,9,1]{3,2,1,0:T(8,128)S(1)} %get-tuple-element.122), channel_id=1, source_target_pairs={{4,0},{8,4},{12,8},{5,1},{9,5},{13,9},{6,2},{10,6},{14,10},{7,3},{... | collective-permute-start | bytes 2924 | tf_op jit(solution)/shard_map/ppermute | solution.py:60
  288.9 5.4 %collective-permute-start.12 = (f32[3,1,9,33]{3,2,1,0:T(8,128)S(1)}, f32[3,1,9,33]{3,2,1,0:T(8,128)S(1)}, u32[]{:S(2)}, u32[]{:S(2)}) collective-permute-start(f32[3,1,9,33]{3,2,1,0:T(8,128)S(1)} %get-tuple-element.171), channel_id=1, source_target_pairs={{0,1},{1,2},{2,3},{4,5},{5,6},{6,7},{8,9},{9,10},{10,11},{12,13},{... | collective-permute-start | bytes 10700 | tf_op jit(solution)/shard_map/ppermute | solution.py:59
  292.8 5.9 %collective-permute-start.13 = (f32[3,1,9,33]{3,2,1,0:T(8,128)S(1)}, f32[3,1,9,33]{3,2,1,0:T(8,128)S(1)}, u32[]{:S(2)}, u32[]{:S(2)}) collective-permute-start(f32[3,1,9,33]{3,2,1,0:T(8,128)S(1)} %get-tuple-element.172), channel_id=1, source_target_pairs={{1,0},{2,1},{3,2},{5,4},{6,5},{7,6},{9,8},{10,9},{11,10},{13,12},{... | collective-permute-start | bytes 10700 | tf_op jit(solution)/shard_map/ppermute | solution.py:60
  298.8 9.7 %collective-permute-start.14 = (f32[3,3,1,33]{3,2,1,0:T(1,128)S(1)}, f32[3,3,1,33]{3,2,1,0:T(1,128)S(1)}, u32[]{:S(2)}, u32[]{:S(2)}) collective-permute-start(f32[3,3,1,33]{3,2,1,0:T(1,128)S(1)} %pad_maximum_fusion.30), channel_id=1, source_target_pairs={{0,16},{16,32},{32,48},{48,64},{64,80},{80,96},{96,112},{112,128},... | collective-permute-start | bytes 3572 | tf_op jit(solution)/shard_map/ppermute | solution.py:59
  308.5 3.2 collective-permute-start.15
  311.9 5.8 %collective-permute-start.16 = (f32[3,3,9,1]{3,2,1,0:T(8,128)S(1)}, f32[3,3,9,1]{3,2,1,0:T(8,128)S(1)}, u32[]{:S(2)}, u32[]{:S(2)}) collective-permute-start(f32[3,3,9,1]{3,2,1,0:T(8,128)S(1)} %get-tuple-element.166), channel_id=1, source_target_pairs={{0,4},{4,8},{8,12},{1,5},{5,9},{9,13},{2,6},{6,10},{10,14},{3,7},{... | collective-permute-start | bytes 980 | tf_op jit(solution)/shard_map/ppermute | solution.py:59
  315.7 6.2 %collective-permute-start.17 = (f32[3,3,9,1]{3,2,1,0:T(8,128)S(1)}, f32[3,3,9,1]{3,2,1,0:T(8,128)S(1)}, u32[]{:S(2)}, u32[]{:S(2)}) collective-permute-start(f32[3,3,9,1]{3,2,1,0:T(8,128)S(1)} %get-tuple-element.167), channel_id=1, source_target_pairs={{4,0},{8,4},{12,8},{5,1},{9,5},{13,9},{6,2},{10,6},{14,10},{7,3},{... | collective-permute-start | bytes 980 | tf_op jit(solution)/shard_map/ppermute | solution.py:60
  337.2 37.0 %copy-start.56 = (f32[1,3,9,33]{3,2,1,0:T(8,128)S(1)}, f32[1,3,9,33]{3,2,1,0:T(8,128)}, u32[]{:S(2)}) copy-start(f32[1,3,9,33]{3,2,1,0:T(8,128)} %copy-done.55) | copy-start | bytes 10696
  337.2 37.0 %copy-start.58 = (f32[1,3,9,33]{3,2,1,0:T(8,128)S(1)}, f32[1,3,9,33]{3,2,1,0:T(8,128)}, u32[]{:S(2)}) copy-start(f32[1,3,9,33]{3,2,1,0:T(8,128)} %copy-done.57) | copy-start | bytes 10696
  337.2 37.0 %copy-start.63 = (f32[3,3,9,33]{3,2,1,0:T(8,128)S(1)}, f32[3,3,9,33]{3,2,1,0:T(8,128)}, u32[]{:S(2)}) copy-start(f32[3,3,9,33]{3,2,1,0:T(8,128)} %get-tuple-element.31) | copy-start | bytes 32080
  341.1 5.1 collective-permute-start.18
  344.8 5.7 %collective-permute-start.19 = (f32[3,1,9,33]{3,2,1,0:T(8,128)S(1)}, f32[3,1,9,33]{3,2,1,0:T(8,128)S(1)}, u32[]{:S(2)}, u32[]{:S(2)}) collective-permute-start(f32[3,1,9,33]{3,2,1,0:T(8,128)S(1)} %get-tuple-element.163), channel_id=1, source_target_pairs={{1,0},{2,1},{3,2},{5,4},{6,5},{7,6},{9,8},{10,9},{11,10},{13,12},{... | collective-permute-start | bytes 10700 | tf_op jit(solution)/shard_map/ppermute | solution.py:60
  350.5 9.7 %collective-permute-start.20 = (f32[3,3,1,33]{3,2,1,0:T(1,128)S(1)}, f32[3,3,1,33]{3,2,1,0:T(1,128)S(1)}, u32[]{:S(2)}, u32[]{:S(2)}) collective-permute-start(f32[3,3,1,33]{3,2,1,0:T(1,128)S(1)} %pad_maximum_fusion.28), channel_id=1, source_target_pairs={{0,16},{16,32},{32,48},{48,64},{64,80},{80,96},{96,112},{112,128},... | collective-permute-start | bytes 3572 | tf_op jit(solution)/shard_map/ppermute | solution.py:59
  360.3 5.4 %collective-permute-start.21 = (f32[3,3,1,33]{3,2,1,0:T(1,128)S(1)}, f32[3,3,1,33]{3,2,1,0:T(1,128)S(1)}, u32[]{:S(2)}, u32[]{:S(2)}) collective-permute-start(f32[3,3,1,33]{3,2,1,0:T(1,128)S(1)} %get-tuple-element.29), channel_id=1, source_target_pairs={{16,0},{32,16},{48,32},{64,48},{80,64},{96,80},{112,96},{128,112},... | collective-permute-start | bytes 3572 | tf_op jit(solution)/shard_map/ppermute | solution.py:60
  365.8 4.1 collective-permute-start.22
  367.8 6.3 %collective-permute-start.23 = (f32[3,3,9,1]{3,2,1,0:T(8,128)S(1)}, f32[3,3,9,1]{3,2,1,0:T(8,128)S(1)}, u32[]{:S(2)}, u32[]{:S(2)}) collective-permute-start(f32[3,3,9,1]{3,2,1,0:T(8,128)S(1)} %get-tuple-element.158), channel_id=1, source_target_pairs={{4,0},{8,4},{12,8},{5,1},{9,5},{13,9},{6,2},{10,6},{14,10},{7,3},{... | collective-permute-start | bytes 980 | tf_op jit(solution)/shard_map/ppermute | solution.py:60
  396.1 3.4 collective-permute-start.24
  398.0 5.7 %collective-permute-start.25 = (f32[3,1,9,33]{3,2,1,0:T(8,128)S(1)}, f32[3,1,9,33]{3,2,1,0:T(8,128)S(1)}, u32[]{:S(2)}, u32[]{:S(2)}) collective-permute-start(f32[3,1,9,33]{3,2,1,0:T(8,128)S(1)} %get-tuple-element.154), channel_id=1, source_target_pairs={{1,0},{2,1},{3,2},{5,4},{6,5},{7,6},{9,8},{10,9},{11,10},{13,12},{... | collective-permute-start | bytes 10700 | tf_op jit(solution)/shard_map/ppermute | solution.py:60
  403.8 9.7 %collective-permute-start.26 = (f32[3,3,1,33]{3,2,1,0:T(1,128)S(1)}, f32[3,3,1,33]{3,2,1,0:T(1,128)S(1)}, u32[]{:S(2)}, u32[]{:S(2)}) collective-permute-start(f32[3,3,1,33]{3,2,1,0:T(1,128)S(1)} %pad_maximum_fusion.26), channel_id=1, source_target_pairs={{0,16},{16,32},{32,48},{48,64},{64,80},{80,96},{96,112},{112,128},... | collective-permute-start | bytes 3572 | tf_op jit(solution)/shard_map/ppermute | solution.py:59
  413.5 3.2 collective-permute-start.27
  416.9 4.2 collective-permute-start.28
  419.1 6.2 %collective-permute-start.29 = (f32[3,3,9,1]{3,2,1,0:T(8,128)S(1)}, f32[3,3,9,1]{3,2,1,0:T(8,128)S(1)}, u32[]{:S(2)}, u32[]{:S(2)}) collective-permute-start(f32[3,3,9,1]{3,2,1,0:T(8,128)S(1)} %get-tuple-element.149), channel_id=1, source_target_pairs={{4,0},{8,4},{12,8},{5,1},{9,5},{13,9},{6,2},{10,6},{14,10},{7,3},{... | collective-permute-start | bytes 980 | tf_op jit(solution)/shard_map/ppermute | solution.py:60
  443.9 3.4 collective-permute-start.30
  445.8 5.7 %collective-permute-start.31 = (f32[3,1,9,33]{3,2,1,0:T(8,128)S(1)}, f32[3,1,9,33]{3,2,1,0:T(8,128)S(1)}, u32[]{:S(2)}, u32[]{:S(2)}) collective-permute-start(f32[3,1,9,33]{3,2,1,0:T(8,128)S(1)} %get-tuple-element.145), channel_id=1, source_target_pairs={{1,0},{2,1},{3,2},{5,4},{6,5},{7,6},{9,8},{10,9},{11,10},{13,12},{... | collective-permute-start | bytes 10700 | tf_op jit(solution)/shard_map/ppermute | solution.py:60
  451.6 9.7 %collective-permute-start.32 = (f32[3,3,1,33]{3,2,1,0:T(1,128)S(1)}, f32[3,3,1,33]{3,2,1,0:T(1,128)S(1)}, u32[]{:S(2)}, u32[]{:S(2)}) collective-permute-start(f32[3,3,1,33]{3,2,1,0:T(1,128)S(1)} %pad_maximum_fusion.24), channel_id=1, source_target_pairs={{0,16},{16,32},{32,48},{48,64},{64,80},{80,96},{96,112},{112,128},... | collective-permute-start | bytes 3572 | tf_op jit(solution)/shard_map/ppermute | solution.py:59
  461.3 3.2 collective-permute-start.33
  464.7 3.9 collective-permute-start.34
  466.6 6.2 %collective-permute-start.35 = (f32[3,3,9,1]{3,2,1,0:T(8,128)S(1)}, f32[3,3,9,1]{3,2,1,0:T(8,128)S(1)}, u32[]{:S(2)}, u32[]{:S(2)}) collective-permute-start(f32[3,3,9,1]{3,2,1,0:T(8,128)S(1)} %get-tuple-element.140), channel_id=1, source_target_pairs={{4,0},{8,4},{12,8},{5,1},{9,5},{13,9},{6,2},{10,6},{14,10},{7,3},{... | collective-permute-start | bytes 980 | tf_op jit(solution)/shard_map/ppermute | solution.py:60
  491.5 3.4 collective-permute-start.36
  493.4 5.7 %collective-permute-start.37 = (f32[3,1,9,33]{3,2,1,0:T(8,128)S(1)}, f32[3,1,9,33]{3,2,1,0:T(8,128)S(1)}, u32[]{:S(2)}, u32[]{:S(2)}) collective-permute-start(f32[3,1,9,33]{3,2,1,0:T(8,128)S(1)} %get-tuple-element.136), channel_id=1, source_target_pairs={{1,0},{2,1},{3,2},{5,4},{6,5},{7,6},{9,8},{10,9},{11,10},{13,12},{... | collective-permute-start | bytes 10700 | tf_op jit(solution)/shard_map/ppermute | solution.py:60
  499.2 9.7 %collective-permute-start.38 = (f32[3,3,1,33]{3,2,1,0:T(1,128)S(1)}, f32[3,3,1,33]{3,2,1,0:T(1,128)S(1)}, u32[]{:S(2)}, u32[]{:S(2)}) collective-permute-start(f32[3,3,1,33]{3,2,1,0:T(1,128)S(1)} %pad_maximum_fusion.22), channel_id=1, source_target_pairs={{0,16},{16,32},{32,48},{48,64},{64,80},{80,96},{96,112},{112,128},... | collective-permute-start | bytes 3572 | tf_op jit(solution)/shard_map/ppermute | solution.py:59
  508.9 3.2 collective-permute-start.39
  512.3 3.9 collective-permute-start.40
  514.2 6.2 %collective-permute-start.41 = (f32[3,3,9,1]{3,2,1,0:T(8,128)S(1)}, f32[3,3,9,1]{3,2,1,0:T(8,128)S(1)}, u32[]{:S(2)}, u32[]{:S(2)}) collective-permute-start(f32[3,3,9,1]{3,2,1,0:T(8,128)S(1)} %get-tuple-element.131), channel_id=1, source_target_pairs={{4,0},{8,4},{12,8},{5,1},{9,5},{13,9},{6,2},{10,6},{14,10},{7,3},{... | collective-permute-start | bytes 980 | tf_op jit(solution)/shard_map/ppermute | solution.py:60
  (74 other events, 711.9 us)
where the time goes:
time: 546 us; the launch traced here: 536 us
  waiting for transfers between devices  167 us (31%)
  local copies, waits for them, and re-layouts  131 us (24%)
  starting transfers between devices  125 us (23%)
  other arithmetic  84.1 us (15%)
  matrix products  17.5 us (3%)
  between operations  10.5 us (2%)
    unnamed x199, local copies, waits for them, and re-layouts  60.4 us
    ppermute x18, waiting for transfers between devices, share(): from_high = lax.ppermute(first, axis, backward)  59.1 us
    ppermute x18, waiting for transfers between devices, share(): from_low = lax.ppermute(last, axis, forward)  47.2 us
    ppermute x18, starting transfers between devices, share(): from_low = lax.ppermute(last, axis, forward)  45.6 us
    ppermute x18, starting transfers between devices, share(): from_high = lax.ppermute(first, axis, backward)  34.2 us
    reduce_sum x7, other arithmetic, reduce_z(): low = jnp.sum(blocks * lower.reshape(shape), axis=2)  21.4 us
    all_to_all x1, waiting for transfers between devices, bricks_of(): lax.all_to_all(deformed_slab, 'gx', split_axis=1, concat_axis=0, tiled=True)  18 us
    ppermute x2, starting transfers between devices, halo(): lax.ppermute(lax.slice_in_dim(block, size - width, size, axis=dim), axis,...  18 us
  transfers between devices with their start and end apart: 44, of which 41 were waited for; matrix products, arithmetic and copies ran while one was open for 3% of the time, Pallas kernels for 0%

commit v1 on v0

--- a/solution.py
+++ b/solution.py
@@ -148,7 +148,11 @@
 
 
 def bricks_of(image_slab, deformed_slab):
-    image = lax.all_to_all(image_slab, "gx", split_axis=1, concat_axis=0, tiled=True)
+    seats_all_enter = lambda sample, bus_axis: jnp.concatenate(
+        lax.all_to_all(jnp.stack(jnp.split(sample, lax.psum(1, bus_axis), 1), 0), bus_axis, 0, 0),
+        axis=0,
+    )
+    image = seats_all_enter(image_slab, "gx")
     deformed = lax.all_to_all(deformed_slab, "gx", split_axis=1, concat_axis=0, tiled=True)
     both = jnp.stack([image, deformed])
     both = halo(both, "gy", 3, DMAX)

time: 546 us -> 387 us (0.71)
  local copies, waits for them, and re-layouts: 131 us -> 31.7 us
  other arithmetic: 84.1 us -> 31 us
  matrix products: 17.5 us -> 11.5 us
    unnamed x199 -> x75, local copies, waits for them, and re-layouts: 60.4 us -> 19.2 us
    slice x18 -> x0, local copies, waits for them, and re-layouts: 19.9 us -> none  [the longest x6 8.43 us: expand_z(): high = values[:, 1:, None]]
    reduce_sum x7, other arithmetic: 21.4 us -> 4.69 us  [reduce_z(): low = jnp.sum(blocks * lower.reshape(shape), axis=2)]
    reduce_sum x4, other arithmetic: 15 us -> 2.53 us  [operator(): inner = jnp.sum(grads * interpolate(delta, tables, weights), axis=0)]
    slice x12 -> x6, local copies, waits for them, and re-layouts: 11.8 us -> 0.44 us  [expand_z(): low = values[:, :count, None]]
    all_to_all x1, waiting for transfers between devices: 18 us -> 9.97 us  [bricks_of(): lax.all_to_all(deformed_slab, 'gx', split_axis=1, concat_axis=0, tiled=True)]
    slice x2 -> x1, local copies, waits for them, and re-layouts: 8.98 us -> 1.53 us  [halo(): lax.slice_in_dim(block, size - width, size, axis=dim)]
    dot_general x7, matrix products: 9.98 us -> 3.26 us  [restrict(): step = jnp.einsum('caxy,xb->caby', step, table_x, precision=HI)]
  transfers between devices with their start and end apart: 44 -> 44, of which waited for: 41 -> 41; matrix products, arithmetic and copies ran while one was open for 3% -> 4% of each run, Pallas kernels for 0% -> 0%
where the time goes in v1:
time: 387 us; the launch traced here: 381 us
  waiting for transfers between devices  169 us (44%)
  starting transfers between devices  128 us (33%)
  local copies, waits for them, and re-layouts  31.7 us (8%)
  other arithmetic  31 us (8%)
  matrix products  11.5 us (3%)
  between operations  10 us (3%)
    ppermute x18, waiting for transfers between devices, share(): from_high = lax.ppermute(first, axis, backward)  59.1 us
    ppermute x18, waiting for transfers between devices, share(): from_low = lax.ppermute(last, axis, forward)  47.9 us
    ppermute x18, starting transfers between devices, share(): from_low = lax.ppermute(last, axis, forward)  43.1 us
    ppermute x18, starting transfers between devices, share(): from_high = lax.ppermute(first, axis, backward)  33.9 us
    unnamed x75, local copies, waits for them, and re-layouts  19.2 us
    all_to_all x1, waiting for transfers between devices, bricks_of(): lax.all_to_all(jnp.stack(jnp.split(sample, lax.psum(1, bus_axis), 1), 0),...  17.8 us
    ppermute x2, starting transfers between devices, halo(): lax.ppermute(lax.slice_in_dim(block, size - width, size, axis=dim), axis,...  16.9 us
    ppermute x2, waiting for transfers between devices, halo(): lax.ppermute(lax.slice_in_dim(block, size - width, size, axis=dim), axis,...  13.2 us
  transfers between devices with their start and end apart: 44, of which 41 were waited for; matrix products, arithmetic and copies ran while one was open for 4% of the time, Pallas kernels for 0%

profile of v1, /device:TPU:4, one launch (start us, length us, event | category | flops | bytes accessed | tf_op | source)
XLA Modules:
  0.0 381.2 jit_solution(16500483398206271821)
XLA Ops:
  0.6 3.4 copy.43
  4.0 11.4 %all-to-all-start.1 = ((f32[1,1024,256]{2,0,1:T(1,128)}), f32[1,1024,256]{2,0,1:T(1,128)S(1)}, u32[]{:S(2)}, u32[]{:S(2)}) async-start(f32[1,1024,256]{2,0,1:T(1,128)} %copy.43), calls=%async_computation.1 | async-start | bytes 2097152 | tf_op jit(solution)/shard_map/all_to_all | solution.py:156
  25.6 10.0 %all-to-all-done.1 = f32[1,1024,256]{2,0,1:T(1,128)S(1)} async-done(((f32[1,1024,256]{2,0,1:T(1,128)}), f32[1,1024,256]{2,0,1:T(1,128)S(1)}, u32[]{:S(2)}, u32[]{:S(2)}) %all-to-all-start.1) | async-done | bytes 1048608 | tf_op jit(solution)/shard_map/all_to_all | solution.py:156
  35.6 6.2 %all-to-all-start = ((f32[16,1,64,256]{3,2,1,0:T(8,128)}), f32[16,1,64,256]{3,2,1,0:T(8,128)S(1)}, u32[]{:S(2)}, u32[]{:S(2)}) async-start(f32[16,1,64,256]{3,2,1,0:T(8,128)} %bitcast_dynamic-update-slice_fusion), calls=%async_computation | async-start | bytes 2097152 | tf_op jit(solution)/shard_map/all_to_all | solution.py:152
  41.8 17.8 %all-to-all-done = f32[16,1,64,256]{3,2,1,0:T(8,128)S(1)} async-done(((f32[16,1,64,256]{3,2,1,0:T(8,128)}), f32[16,1,64,256]{3,2,1,0:T(8,128)S(1)}, u32[]{:S(2)}, u32[]{:S(2)}) %all-to-all-start) | async-done | bytes 1048608 | tf_op jit(solution)/shard_map/all_to_all | solution.py:152
  62.6 15.0 %collective-permute-start = (f32[2,16,64,8]{2,3,1,0:T(8,128)S(1)}, f32[2,16,64,8]{2,3,1,0:T(8,128)S(1)}, u32[]{:S(2)}, u32[]{:S(2)}) collective-permute-start(f32[2,16,64,8]{2,3,1,0:T(8,128)S(1)} %copy.44), channel_id=1, source_target_pairs={{0,4},{4,8},{8,12},{1,5},{5,9},{9,13},{2,6},{6,10},{10,14},{3,7},{... | collective-permute-start | bytes 196616 | tf_op jit(solution)/shard_map/ppermute | solution.py:47
  80.9 5.1 %collective-permute-done.1 = f32[2,16,64,8]{2,3,1,0:T(8,128)} collective-permute-done((f32[2,16,64,8]{2,3,1,0:T(8,128)}, f32[2,16,64,8]{2,3,1,0:T(8,128)}, u32[]{:S(2)}, u32[]{:S(2)}) %collective-permute-start.1) | collective-permute-done | bytes 65568 | tf_op jit(solution)/shard_map/ppermute | solution.py:48
  85.9 2.2 copy.47
  89.5 1.9 collective-permute-start.2
  91.5 8.4 %collective-permute-start.3 = (f32[2,16,8,272]{3,2,1,0:T(8,128)S(1)}, f32[2,16,8,272]{3,2,1,0:T(8,128)S(1)}, u32[]{:S(2)}, u32[]{:S(2)}) collective-permute-start(f32[2,16,8,272]{3,2,1,0:T(8,128)S(1)} %get-tuple-element.51), channel_id=1, source_target_pairs={{16,0},{32,16},{48,32},{64,48},{80,64},{96,80},{112,96},{128,112},... | collective-permute-start | bytes 835592 | tf_op jit(solution)/shard_map/ppermute | solution.py:48
  99.9 12.5 %collective-permute-done.2 = f32[2,16,8,272]{3,2,1,0:T(8,128)S(1)} collective-permute-done((f32[2,16,8,272]{3,2,1,0:T(8,128)S(1)}, f32[2,16,8,272]{3,2,1,0:T(8,128)S(1)}, u32[]{:S(2)}, u32[]{:S(2)}) %collective-permute-start.2) | collective-permute-done | bytes 278560 | tf_op jit(solution)/shard_map/ppermute | solution.py:47
  118.7 5.1 %collective-permute-start.5 = (f32[9,80,272]{2,1,0:T(8,128)}, f32[9,80,272]{2,1,0:T(8,128)S(1)}, u32[]{:S(2)}, u32[]{:S(2)}) collective-permute-start(f32[9,80,272]{2,1,0:T(8,128)} %pad_maximum_fusion.7), channel_id=1, source_target_pairs={{0,1},{1,2},{2,3},{4,5},{5,6},{6,7},{8,9},{9,10},{10,11},{12,13},{... | collective-permute-start | bytes 2350088 | tf_op jit(solution)/shard_map/ppermute | solution.py:166
  129.0 2.4 slice_bitcast_fusion
  131.4 13.0 %collective-permute-done.4 = f32[9,80,272]{2,1,0:T(8,128)S(1)} collective-permute-done((f32[9,80,272]{2,1,0:T(8,128)S(1)}, f32[9,80,272]{2,1,0:T(8,128)S(1)}, u32[]{:S(2)}, u32[]{:S(2)}) %collective-permute-start.4) | collective-permute-done | bytes 783392 | tf_op jit(solution)/shard_map/ppermute | solution.py:167
  144.4 3.1 collective-permute-done.5
  162.2 4.3 %collective-permute-start.6 = (f32[9,1,9,33]{3,2,1,0:T(8,128)S(1)}, f32[9,1,9,33]{3,2,1,0:T(8,128)S(1)}, u32[]{:S(2)}, u32[]{:S(2)}) collective-permute-start(f32[9,1,9,33]{3,2,1,0:T(8,128)S(1)} %fusion.61), channel_id=1, source_target_pairs={{0,1},{1,2},{2,3},{4,5},{5,6},{6,7},{8,9},{9,10},{10,11},{12,13},{... | collective-permute-start | bytes 32084 | tf_op jit(solution)/shard_map/ppermute | solution.py:59
  166.5 2.3 collective-permute-done.6
  170.2 5.4 %collective-permute-done.7 = f32[9,1,9,33]{3,2,1,0:T(8,128)S(1)} collective-permute-done((f32[9,1,9,33]{3,2,1,0:T(8,128)S(1)}, f32[9,1,9,33]{3,2,1,0:T(8,128)S(1)}, u32[]{:S(2)}, u32[]{:S(2)}) %collective-permute-start.7) | collective-permute-done | bytes 10724 | tf_op jit(solution)/shard_map/ppermute | solution.py:60
  177.6 8.4 %collective-permute-start.9 = (f32[9,3,1,33]{3,2,1,0:T(1,128)S(1)}, f32[9,3,1,33]{3,2,1,0:T(1,128)S(1)}, u32[]{:S(2)}, u32[]{:S(2)}) collective-permute-start(f32[9,3,1,33]{3,2,1,0:T(1,128)S(1)} %get-tuple-element.119), channel_id=1, source_target_pairs={{16,0},{32,16},{48,32},{64,48},{80,64},{96,80},{112,96},{128,112},... | collective-permute-start | bytes 10700 | tf_op jit(solution)/shard_map/ppermute | solution.py:60
  187.6 2.9 collective-permute-start.10
  192.1 3.0 collective-permute-done.10
  195.1 4.1 %collective-permute-done.11 = f32[9,3,9,1]{3,2,1,0:T(8,128)S(1)} collective-permute-done((f32[9,3,9,1]{3,2,1,0:T(8,128)S(1)}, f32[9,3,9,1]{3,2,1,0:T(8,128)S(1)}, u32[]{:S(2)}, u32[]{:S(2)}) %collective-permute-start.11) | collective-permute-done | bytes 1004 | tf_op jit(solution)/shard_map/ppermute | solution.py:60
  203.0 3.9 %collective-permute-start.12 = (f32[3,1,9,33]{3,2,1,0:T(8,128)S(1)}, f32[3,1,9,33]{3,2,1,0:T(8,128)S(1)}, u32[]{:S(2)}, u32[]{:S(2)}) collective-permute-start(f32[3,1,9,33]{3,2,1,0:T(8,128)S(1)} %get-tuple-element.164), channel_id=1, source_target_pairs={{0,1},{1,2},{2,3},{4,5},{5,6},{6,7},{8,9},{9,10},{10,11},{12,13},{... | collective-permute-start | bytes 10700 | tf_op jit(solution)/shard_map/ppermute | solution.py:59
  208.4 4.2 %collective-permute-done.13 = f32[3,1,9,33]{3,2,1,0:T(8,128)S(1)} collective-permute-done((f32[3,1,9,33]{3,2,1,0:T(8,128)S(1)}, f32[3,1,9,33]{3,2,1,0:T(8,128)S(1)}, u32[]{:S(2)}, u32[]{:S(2)}) %collective-permute-start.13) | collective-permute-done | bytes 3596 | tf_op jit(solution)/shard_map/ppermute | solution.py:60
  214.6 7.8 %collective-permute-done.14 = f32[3,3,1,33]{3,2,1,0:T(1,128)S(1)} collective-permute-done((f32[3,3,1,33]{3,2,1,0:T(1,128)S(1)}, f32[3,3,1,33]{3,2,1,0:T(1,128)S(1)}, u32[]{:S(2)}, u32[]{:S(2)}) %collective-permute-start.14) | collective-permute-done | bytes 1220 | tf_op jit(solution)/shard_map/ppermute | solution.py:59
  225.7 3.0 collective-permute-start.16
  230.8 4.3 %collective-permute-done.17 = f32[3,3,9,1]{3,2,1,0:T(8,128)S(1)} collective-permute-done((f32[3,3,9,1]{3,2,1,0:T(8,128)S(1)}, f32[3,3,9,1]{3,2,1,0:T(8,128)S(1)}, u32[]{:S(2)}, u32[]{:S(2)}) %collective-permute-start.17) | collective-permute-done | bytes 356 | tf_op jit(solution)/shard_map/ppermute | solution.py:60
  239.3 3.5 collective-permute-start.18
  244.3 4.2 %collective-permute-done.19 = f32[3,1,9,33]{3,2,1,0:T(8,128)S(1)} collective-permute-done((f32[3,1,9,33]{3,2,1,0:T(8,128)S(1)}, f32[3,1,9,33]{3,2,1,0:T(8,128)S(1)}, u32[]{:S(2)}, u32[]{:S(2)}) %collective-permute-start.19) | collective-permute-done | bytes 3596 | tf_op jit(solution)/shard_map/ppermute | solution.py:60
  248.6 1.9 collective-permute-start.20
  250.5 7.8 %collective-permute-done.20 = f32[3,3,1,33]{3,2,1,0:T(1,128)S(1)} collective-permute-done((f32[3,3,1,33]{3,2,1,0:T(1,128)S(1)}, f32[3,3,1,33]{3,2,1,0:T(1,128)S(1)}, u32[]{:S(2)}, u32[]{:S(2)}) %collective-permute-start.20) | collective-permute-done | bytes 1220 | tf_op jit(solution)/shard_map/ppermute | solution.py:59
  258.4 1.9 collective-permute-start.21
  265.5 2.8 collective-permute-start.22
  270.1 4.7 %collective-permute-done.23 = f32[3,3,9,1]{3,2,1,0:T(8,128)} collective-permute-done((f32[3,3,9,1]{3,2,1,0:T(8,128)}, f32[3,3,9,1]{3,2,1,0:T(8,128)}, u32[]{:S(2)}, u32[]{:S(2)}) %collective-permute-start.23) | collective-permute-done | bytes 356 | tf_op jit(solution)/shard_map/ppermute | solution.py:60
  283.3 2.0 collective-permute-start.24
  286.8 4.2 %collective-permute-done.25 = f32[3,1,9,33]{3,2,1,0:T(8,128)S(1)} collective-permute-done((f32[3,1,9,33]{3,2,1,0:T(8,128)S(1)}, f32[3,1,9,33]{3,2,1,0:T(8,128)S(1)}, u32[]{:S(2)}, u32[]{:S(2)}) %collective-permute-start.25) | collective-permute-done | bytes 3596 | tf_op jit(solution)/shard_map/ppermute | solution.py:60
  291.1 1.9 collective-permute-start.26
  293.0 7.8 %collective-permute-done.26 = f32[3,3,1,33]{3,2,1,0:T(1,128)S(1)} collective-permute-done((f32[3,3,1,33]{3,2,1,0:T(1,128)S(1)}, f32[3,3,1,33]{3,2,1,0:T(1,128)S(1)}, u32[]{:S(2)}, u32[]{:S(2)}) %collective-permute-start.26) | collective-permute-done | bytes 1220 | tf_op jit(solution)/shard_map/ppermute | solution.py:59
  300.8 1.9 collective-permute-start.27
  307.7 4.3 %collective-permute-done.29 = f32[3,3,9,1]{3,2,1,0:T(8,128)S(1)} collective-permute-done((f32[3,3,9,1]{3,2,1,0:T(8,128)S(1)}, f32[3,3,9,1]{3,2,1,0:T(8,128)S(1)}, u32[]{:S(2)}, u32[]{:S(2)}) %collective-permute-start.29) | collective-permute-done | bytes 356 | tf_op jit(solution)/shard_map/ppermute | solution.py:60
  318.7 4.2 %collective-permute-done.31 = f32[3,1,9,33]{3,2,1,0:T(8,128)S(1)} collective-permute-done((f32[3,1,9,33]{3,2,1,0:T(8,128)S(1)}, f32[3,1,9,33]{3,2,1,0:T(8,128)S(1)}, u32[]{:S(2)}, u32[]{:S(2)}) %collective-permute-start.31) | collective-permute-done | bytes 3596 | tf_op jit(solution)/shard_map/ppermute | solution.py:60
  324.9 7.8 %collective-permute-done.32 = f32[3,3,1,33]{3,2,1,0:T(1,128)S(1)} collective-permute-done((f32[3,3,1,33]{3,2,1,0:T(1,128)S(1)}, f32[3,3,1,33]{3,2,1,0:T(1,128)S(1)}, u32[]{:S(2)}, u32[]{:S(2)}) %collective-permute-start.32) | collective-permute-done | bytes 1220 | tf_op jit(solution)/shard_map/ppermute | solution.py:59
  336.1 1.9 collective-permute-start.34
  340.0 4.3 %collective-permute-done.35 = f32[3,3,9,1]{3,2,1,0:T(8,128)S(1)} collective-permute-done((f32[3,3,9,1]{3,2,1,0:T(8,128)S(1)}, f32[3,3,9,1]{3,2,1,0:T(8,128)S(1)}, u32[]{:S(2)}, u32[]{:S(2)}) %collective-permute-start.35) | collective-permute-done | bytes 356 | tf_op jit(solution)/shard_map/ppermute | solution.py:60
  347.6 1.9 collective-permute-start.36
  351.0 4.2 %collective-permute-done.37 = f32[3,1,9,33]{3,2,1,0:T(8,128)S(1)} collective-permute-done((f32[3,1,9,33]{3,2,1,0:T(8,128)S(1)}, f32[3,1,9,33]{3,2,1,0:T(8,128)S(1)}, u32[]{:S(2)}, u32[]{:S(2)}) %collective-permute-start.37) | collective-permute-done | bytes 3596 | tf_op jit(solution)/shard_map/ppermute | solution.py:60
  357.2 7.8 %collective-permute-done.38 = f32[3,3,1,33]{3,2,1,0:T(1,128)S(1)} collective-permute-done((f32[3,3,1,33]{3,2,1,0:T(1,128)S(1)}, f32[3,3,1,33]{3,2,1,0:T(1,128)S(1)}, u32[]{:S(2)}, u32[]{:S(2)}) %collective-permute-start.38) | collective-permute-done | bytes 1220 | tf_op jit(solution)/shard_map/ppermute | solution.py:59
  372.3 4.3 %collective-permute-done.41 = f32[3,3,9,1]{3,2,1,0:T(8,128)S(1)} collective-permute-done((f32[3,3,9,1]{3,2,1,0:T(8,128)S(1)}, f32[3,3,9,1]{3,2,1,0:T(8,128)S(1)}, u32[]{:S(2)}, u32[]{:S(2)}) %collective-permute-start.41) | collective-permute-done | bytes 356 | tf_op jit(solution)/shard_map/ppermute | solution.py:60
  (280 shorter events, 114.4 us)
Async XLA Ops:
  4.0 31.6 %all-to-all-start.1 = ((f32[1,1024,256]{2,0,1:T(1,128)}), f32[1,1024,256]{2,0,1:T(1,128)S(1)}, u32[]{:S(2)}, u32[]{:S(2)}) async-start(f32[1,1024,256]{2,0,1:T(1,128)} %copy.43), calls=%async_computation.1 | async-start | bytes 2097152 | tf_op jit(solution)/shard_map/all_to_all | solution.py:156
  35.6 24.1 %all-to-all-start = ((f32[16,1,64,256]{3,2,1,0:T(8,128)}), f32[16,1,64,256]{3,2,1,0:T(8,128)S(1)}, u32[]{:S(2)}, u32[]{:S(2)}) async-start(f32[16,1,64,256]{3,2,1,0:T(8,128)} %bitcast_dynamic-update-slice_fusion), calls=%async_computation | async-start | bytes 2097152 | tf_op jit(solution)/shard_map/all_to_all | solution.py:152
  62.6 17.9 %collective-permute-start = (f32[2,16,64,8]{2,3,1,0:T(8,128)S(1)}, f32[2,16,64,8]{2,3,1,0:T(8,128)S(1)}, u32[]{:S(2)}, u32[]{:S(2)}) collective-permute-start(f32[2,16,64,8]{2,3,1,0:T(8,128)S(1)} %copy.44), channel_id=1, source_target_pairs={{0,4},{4,8},{8,12},{1,5},{5,9},{9,13},{2,6},{6,10},{10,14},{3,7},{... | collective-permute-start | bytes 196616 | tf_op jit(solution)/shard_map/ppermute | solution.py:47
  78.6 7.3 %collective-permute-start.1 = (f32[2,16,64,8]{2,3,1,0:T(8,128)}, f32[2,16,64,8]{2,3,1,0:T(8,128)}, u32[]{:S(2)}, u32[]{:S(2)}) collective-permute-start(f32[2,16,64,8]{2,3,1,0:T(8,128)} %copy.45), channel_id=1, source_target_pairs={{4,0},{8,4},{12,8},{5,1},{9,5},{13,9},{6,2},{10,6},{14,10},{7,3},{... | collective-permute-start | bytes 196616 | tf_op jit(solution)/shard_map/ppermute | solution.py:48
  89.5 22.9 %collective-permute-start.2 = (f32[2,16,8,272]{3,2,1,0:T(8,128)S(1)}, f32[2,16,8,272]{3,2,1,0:T(8,128)S(1)}, u32[]{:S(2)}, u32[]{:S(2)}) collective-permute-start(f32[2,16,8,272]{3,2,1,0:T(8,128)S(1)} %get-tuple-element.50), channel_id=1, source_target_pairs={{0,16},{16,32},{32,48},{48,64},{64,80},{80,96},{96,112},{112,128},... | collective-permute-start | bytes 835592 | tf_op jit(solution)/shard_map/ppermute | solution.py:47
  91.5 21.0 %collective-permute-start.3 = (f32[2,16,8,272]{3,2,1,0:T(8,128)S(1)}, f32[2,16,8,272]{3,2,1,0:T(8,128)S(1)}, u32[]{:S(2)}, u32[]{:S(2)}) collective-permute-start(f32[2,16,8,272]{3,2,1,0:T(8,128)S(1)} %get-tuple-element.51), channel_id=1, source_target_pairs={{16,0},{32,16},{48,32},{64,48},{80,64},{96,80},{112,96},{128,112},... | collective-permute-start | bytes 835592 | tf_op jit(solution)/shard_map/ppermute | solution.py:48
  116.3 28.0 %collective-permute-start.4 = (f32[9,80,272]{2,1,0:T(8,128)S(1)}, f32[9,80,272]{2,1,0:T(8,128)S(1)}, u32[]{:S(2)}, u32[]{:S(2)}) collective-permute-start(f32[9,80,272]{2,1,0:T(8,128)S(1)} %pad_maximum_fusion.6), channel_id=1, source_target_pairs={{1,0},{2,1},{3,2},{5,4},{6,5},{7,6},{9,8},{10,9},{11,10},{13,12},{... | collective-permute-start | bytes 2350088 | tf_op jit(solution)/shard_map/ppermute | solution.py:167
  118.7 28.8 %collective-permute-start.5 = (f32[9,80,272]{2,1,0:T(8,128)}, f32[9,80,272]{2,1,0:T(8,128)S(1)}, u32[]{:S(2)}, u32[]{:S(2)}) collective-permute-start(f32[9,80,272]{2,1,0:T(8,128)} %pad_maximum_fusion.7), channel_id=1, source_target_pairs={{0,1},{1,2},{2,3},{4,5},{5,6},{6,7},{8,9},{9,10},{10,11},{12,13},{... | collective-permute-start | bytes 2350088 | tf_op jit(solution)/shard_map/ppermute | solution.py:166
  131.4 24.8 %copy-start = (f32[16,80,272]{2,1,0:T(8,128)}, f32[16,80,272]{2,1,0:T(8,128)S(1)}, u32[]{:S(2)}) copy-start(f32[16,80,272]{2,1,0:T(8,128)S(1)} %get-tuple-element.53) | copy-start | bytes 4177924
  161.8 37.7 %copy-start.22 = (f32[6]{0:T(128)S(1)}, f32[6]{0:T(128)}, u32[]{:S(2)}) copy-start(f32[6]{0:T(128)} %constant.84) | copy-start | bytes 76
  162.2 6.6 %collective-permute-start.6 = (f32[9,1,9,33]{3,2,1,0:T(8,128)S(1)}, f32[9,1,9,33]{3,2,1,0:T(8,128)S(1)}, u32[]{:S(2)}, u32[]{:S(2)}) collective-permute-start(f32[9,1,9,33]{3,2,1,0:T(8,128)S(1)} %fusion.61), channel_id=1, source_target_pairs={{0,1},{1,2},{2,3},{4,5},{5,6},{6,7},{8,9},{9,10},{10,11},{12,13},{... | collective-permute-start | bytes 32084 | tf_op jit(solution)/shard_map/ppermute | solution.py:59
  168.9 6.7 %collective-permute-start.7 = (f32[9,1,9,33]{3,2,1,0:T(8,128)S(1)}, f32[9,1,9,33]{3,2,1,0:T(8,128)S(1)}, u32[]{:S(2)}, u32[]{:S(2)}) collective-permute-start(f32[9,1,9,33]{3,2,1,0:T(8,128)S(1)} %get-tuple-element.42), channel_id=1, source_target_pairs={{1,0},{2,1},{3,2},{5,4},{6,5},{7,6},{9,8},{10,9},{11,10},{13,12},{... | collective-permute-start | bytes 32084 | tf_op jit(solution)/shard_map/ppermute | solution.py:60
  175.6 10.4 %collective-permute-start.8 = (f32[9,3,1,33]{3,2,1,0:T(1,128)S(1)}, f32[9,3,1,33]{3,2,1,0:T(1,128)S(1)}, u32[]{:S(2)}, u32[]{:S(2)}) collective-permute-start(f32[9,3,1,33]{3,2,1,0:T(1,128)S(1)} %get-tuple-element.118), channel_id=1, source_target_pairs={{0,16},{16,32},{32,48},{48,64},{64,80},{80,96},{96,112},{112,128},... | collective-permute-start | bytes 10700 | tf_op jit(solution)/shard_map/ppermute | solution.py:59
  177.6 9.9 %collective-permute-start.9 = (f32[9,3,1,33]{3,2,1,0:T(1,128)S(1)}, f32[9,3,1,33]{3,2,1,0:T(1,128)S(1)}, u32[]{:S(2)}, u32[]{:S(2)}) collective-permute-start(f32[9,3,1,33]{3,2,1,0:T(1,128)S(1)} %get-tuple-element.119), channel_id=1, source_target_pairs={{16,0},{32,16},{48,32},{64,48},{80,64},{96,80},{112,96},{128,112},... | collective-permute-start | bytes 10700 | tf_op jit(solution)/shard_map/ppermute | solution.py:60
  187.6 7.5 %collective-permute-start.10 = (f32[9,3,9,1]{3,2,1,0:T(8,128)S(1)}, f32[9,3,9,1]{3,2,1,0:T(8,128)S(1)}, u32[]{:S(2)}, u32[]{:S(2)}) collective-permute-start(f32[9,3,9,1]{3,2,1,0:T(8,128)S(1)} %get-tuple-element.114), channel_id=1, source_target_pairs={{0,4},{4,8},{8,12},{1,5},{5,9},{9,13},{2,6},{6,10},{10,14},{3,7},{... | collective-permute-start | bytes 2924 | tf_op jit(solution)/shard_map/ppermute | solution.py:59
  190.5 8.7 %collective-permute-start.11 = (f32[9,3,9,1]{3,2,1,0:T(8,128)S(1)}, f32[9,3,9,1]{3,2,1,0:T(8,128)S(1)}, u32[]{:S(2)}, u32[]{:S(2)}) collective-permute-start(f32[9,3,9,1]{3,2,1,0:T(8,128)S(1)} %get-tuple-element.115), channel_id=1, source_target_pairs={{4,0},{8,4},{12,8},{5,1},{9,5},{13,9},{6,2},{10,6},{14,10},{7,3},{... | collective-permute-start | bytes 2924 | tf_op jit(solution)/shard_map/ppermute | solution.py:60
  203.0 5.4 %collective-permute-start.12 = (f32[3,1,9,33]{3,2,1,0:T(8,128)S(1)}, f32[3,1,9,33]{3,2,1,0:T(8,128)S(1)}, u32[]{:S(2)}, u32[]{:S(2)}) collective-permute-start(f32[3,1,9,33]{3,2,1,0:T(8,128)S(1)} %get-tuple-element.164), channel_id=1, source_target_pairs={{0,1},{1,2},{2,3},{4,5},{5,6},{6,7},{8,9},{9,10},{10,11},{12,13},{... | collective-permute-start | bytes 10700 | tf_op jit(solution)/shard_map/ppermute | solution.py:59
  206.9 5.7 %collective-permute-start.13 = (f32[3,1,9,33]{3,2,1,0:T(8,128)S(1)}, f32[3,1,9,33]{3,2,1,0:T(8,128)S(1)}, u32[]{:S(2)}, u32[]{:S(2)}) collective-permute-start(f32[3,1,9,33]{3,2,1,0:T(8,128)S(1)} %get-tuple-element.165), channel_id=1, source_target_pairs={{1,0},{2,1},{3,2},{5,4},{6,5},{7,6},{9,8},{10,9},{11,10},{13,12},{... | collective-permute-start | bytes 10700 | tf_op jit(solution)/shard_map/ppermute | solution.py:60
  212.6 9.7 %collective-permute-start.14 = (f32[3,3,1,33]{3,2,1,0:T(1,128)S(1)}, f32[3,3,1,33]{3,2,1,0:T(1,128)S(1)}, u32[]{:S(2)}, u32[]{:S(2)}) collective-permute-start(f32[3,3,1,33]{3,2,1,0:T(1,128)S(1)} %pad_maximum_fusion.32), channel_id=1, source_target_pairs={{0,16},{16,32},{32,48},{48,64},{64,80},{80,96},{96,112},{112,128},... | collective-permute-start | bytes 3572 | tf_op jit(solution)/shard_map/ppermute | solution.py:59
  222.4 3.2 collective-permute-start.15
  225.7 5.0 %collective-permute-start.16 = (f32[3,3,9,1]{3,2,1,0:T(8,128)S(1)}, f32[3,3,9,1]{3,2,1,0:T(8,128)S(1)}, u32[]{:S(2)}, u32[]{:S(2)}) collective-permute-start(f32[3,3,9,1]{3,2,1,0:T(8,128)S(1)} %get-tuple-element.159), channel_id=1, source_target_pairs={{0,4},{4,8},{8,12},{1,5},{5,9},{9,13},{2,6},{6,10},{10,14},{3,7},{... | collective-permute-start | bytes 980 | tf_op jit(solution)/shard_map/ppermute | solution.py:59
  228.8 6.2 %collective-permute-start.17 = (f32[3,3,9,1]{3,2,1,0:T(8,128)S(1)}, f32[3,3,9,1]{3,2,1,0:T(8,128)S(1)}, u32[]{:S(2)}, u32[]{:S(2)}) collective-permute-start(f32[3,3,9,1]{3,2,1,0:T(8,128)S(1)} %get-tuple-element.160), channel_id=1, source_target_pairs={{4,0},{8,4},{12,8},{5,1},{9,5},{13,9},{6,2},{10,6},{14,10},{7,3},{... | collective-permute-start | bytes 980 | tf_op jit(solution)/shard_map/ppermute | solution.py:60
  239.3 5.0 %collective-permute-start.18 = (f32[3,1,9,33]{3,2,1,0:T(8,128)S(1)}, f32[3,1,9,33]{3,2,1,0:T(8,128)S(1)}, u32[]{:S(2)}, u32[]{:S(2)}) collective-permute-start(f32[3,1,9,33]{3,2,1,0:T(8,128)S(1)} %get-tuple-element.155), channel_id=1, source_target_pairs={{0,1},{1,2},{2,3},{4,5},{5,6},{6,7},{8,9},{9,10},{10,11},{12,13},{... | collective-permute-start | bytes 10700 | tf_op jit(solution)/shard_map/ppermute | solution.py:59
  242.8 5.7 %collective-permute-start.19 = (f32[3,1,9,33]{3,2,1,0:T(8,128)S(1)}, f32[3,1,9,33]{3,2,1,0:T(8,128)S(1)}, u32[]{:S(2)}, u32[]{:S(2)}) collective-permute-start(f32[3,1,9,33]{3,2,1,0:T(8,128)S(1)} %get-tuple-element.156), channel_id=1, source_target_pairs={{1,0},{2,1},{3,2},{5,4},{6,5},{7,6},{9,8},{10,9},{11,10},{13,12},{... | collective-permute-start | bytes 10700 | tf_op jit(solution)/shard_map/ppermute | solution.py:60
  248.6 9.7 %collective-permute-start.20 = (f32[3,3,1,33]{3,2,1,0:T(1,128)S(1)}, f32[3,3,1,33]{3,2,1,0:T(1,128)S(1)}, u32[]{:S(2)}, u32[]{:S(2)}) collective-permute-start(f32[3,3,1,33]{3,2,1,0:T(1,128)S(1)} %pad_maximum_fusion.30), channel_id=1, source_target_pairs={{0,16},{16,32},{32,48},{48,64},{64,80},{80,96},{96,112},{112,128},... | collective-permute-start | bytes 3572 | tf_op jit(solution)/shard_map/ppermute | solution.py:59
  258.4 5.6 %collective-permute-start.21 = (f32[3,3,1,33]{3,2,1,0:T(1,128)S(1)}, f32[3,3,1,33]{3,2,1,0:T(1,128)S(1)}, u32[]{:S(2)}, u32[]{:S(2)}) collective-permute-start(f32[3,3,1,33]{3,2,1,0:T(1,128)S(1)} %get-tuple-element.29), channel_id=1, source_target_pairs={{16,0},{32,16},{48,32},{64,48},{80,64},{96,80},{112,96},{128,112},... | collective-permute-start | bytes 3572 | tf_op jit(solution)/shard_map/ppermute | solution.py:60
  265.5 4.6 %collective-permute-start.22 = (f32[3,3,9,1]{3,2,1,0:T(8,128)}, f32[3,3,9,1]{3,2,1,0:T(8,128)}, u32[]{:S(2)}, u32[]{:S(2)}) collective-permute-start(f32[3,3,9,1]{3,2,1,0:T(8,128)} %get-tuple-element.150), channel_id=1, source_target_pairs={{0,4},{4,8},{8,12},{1,5},{5,9},{9,13},{2,6},{6,10},{10,14},{3,7},{... | collective-permute-start | bytes 980 | tf_op jit(solution)/shard_map/ppermute | solution.py:59
  268.3 6.6 %collective-permute-start.23 = (f32[3,3,9,1]{3,2,1,0:T(8,128)}, f32[3,3,9,1]{3,2,1,0:T(8,128)}, u32[]{:S(2)}, u32[]{:S(2)}) collective-permute-start(f32[3,3,9,1]{3,2,1,0:T(8,128)} %get-tuple-element.151), channel_id=1, source_target_pairs={{4,0},{8,4},{12,8},{5,1},{9,5},{13,9},{6,2},{10,6},{14,10},{7,3},{... | collective-permute-start | bytes 980 | tf_op jit(solution)/shard_map/ppermute | solution.py:60
  283.3 3.5 collective-permute-start.24
  285.3 5.7 %collective-permute-start.25 = (f32[3,1,9,33]{3,2,1,0:T(8,128)S(1)}, f32[3,1,9,33]{3,2,1,0:T(8,128)S(1)}, u32[]{:S(2)}, u32[]{:S(2)}) collective-permute-start(f32[3,1,9,33]{3,2,1,0:T(8,128)S(1)} %get-tuple-element.147), channel_id=1, source_target_pairs={{1,0},{2,1},{3,2},{5,4},{6,5},{7,6},{9,8},{10,9},{11,10},{13,12},{... | collective-permute-start | bytes 10700 | tf_op jit(solution)/shard_map/ppermute | solution.py:60
  291.1 9.7 %collective-permute-start.26 = (f32[3,3,1,33]{3,2,1,0:T(1,128)S(1)}, f32[3,3,1,33]{3,2,1,0:T(1,128)S(1)}, u32[]{:S(2)}, u32[]{:S(2)}) collective-permute-start(f32[3,3,1,33]{3,2,1,0:T(1,128)S(1)} %pad_maximum_fusion.28), channel_id=1, source_target_pairs={{0,16},{16,32},{32,48},{48,64},{64,80},{80,96},{96,112},{112,128},... | collective-permute-start | bytes 3572 | tf_op jit(solution)/shard_map/ppermute | solution.py:59
  300.8 3.2 collective-permute-start.27
  304.2 3.5 collective-permute-start.28
  305.7 6.2 %collective-permute-start.29 = (f32[3,3,9,1]{3,2,1,0:T(8,128)S(1)}, f32[3,3,9,1]{3,2,1,0:T(8,128)S(1)}, u32[]{:S(2)}, u32[]{:S(2)}) collective-permute-start(f32[3,3,9,1]{3,2,1,0:T(8,128)S(1)} %get-tuple-element.142), channel_id=1, source_target_pairs={{4,0},{8,4},{12,8},{5,1},{9,5},{13,9},{6,2},{10,6},{14,10},{7,3},{... | collective-permute-start | bytes 980 | tf_op jit(solution)/shard_map/ppermute | solution.py:60
  315.3 3.4 collective-permute-start.30
  317.2 5.7 %collective-permute-start.31 = (f32[3,1,9,33]{3,2,1,0:T(8,128)S(1)}, f32[3,1,9,33]{3,2,1,0:T(8,128)S(1)}, u32[]{:S(2)}, u32[]{:S(2)}) collective-permute-start(f32[3,1,9,33]{3,2,1,0:T(8,128)S(1)} %get-tuple-element.138), channel_id=1, source_target_pairs={{1,0},{2,1},{3,2},{5,4},{6,5},{7,6},{9,8},{10,9},{11,10},{13,12},{... | collective-permute-start | bytes 10700 | tf_op jit(solution)/shard_map/ppermute | solution.py:60
  323.0 9.7 %collective-permute-start.32 = (f32[3,3,1,33]{3,2,1,0:T(1,128)S(1)}, f32[3,3,1,33]{3,2,1,0:T(1,128)S(1)}, u32[]{:S(2)}, u32[]{:S(2)}) collective-permute-start(f32[3,3,1,33]{3,2,1,0:T(1,128)S(1)} %pad_maximum_fusion.26), channel_id=1, source_target_pairs={{0,16},{16,32},{32,48},{48,64},{64,80},{80,96},{96,112},{112,128},... | collective-permute-start | bytes 3572 | tf_op jit(solution)/shard_map/ppermute | solution.py:59
  332.7 3.2 collective-permute-start.33
  336.1 3.9 %collective-permute-start.34 = (f32[3,3,9,1]{3,2,1,0:T(8,128)S(1)}, f32[3,3,9,1]{3,2,1,0:T(8,128)S(1)}, u32[]{:S(2)}, u32[]{:S(2)}) collective-permute-start(f32[3,3,9,1]{3,2,1,0:T(8,128)S(1)} %get-tuple-element.132), channel_id=1, source_target_pairs={{0,4},{4,8},{8,12},{1,5},{5,9},{9,13},{2,6},{6,10},{10,14},{3,7},{... | collective-permute-start | bytes 980 | tf_op jit(solution)/shard_map/ppermute | solution.py:59
  338.0 6.2 %collective-permute-start.35 = (f32[3,3,9,1]{3,2,1,0:T(8,128)S(1)}, f32[3,3,9,1]{3,2,1,0:T(8,128)S(1)}, u32[]{:S(2)}, u32[]{:S(2)}) collective-permute-start(f32[3,3,9,1]{3,2,1,0:T(8,128)S(1)} %get-tuple-element.133), channel_id=1, source_target_pairs={{4,0},{8,4},{12,8},{5,1},{9,5},{13,9},{6,2},{10,6},{14,10},{7,3},{... | collective-permute-start | bytes 980 | tf_op jit(solution)/shard_map/ppermute | solution.py:60
  346.8 30.0 %copy-start.12 = (f32[1,3,9,33]{3,2,1,0:T(8,128)S(1)}, f32[1,3,9,33]{3,2,1,0:T(8,128)}, u32[]{:S(2)}) copy-start(f32[1,3,9,33]{3,2,1,0:T(8,128)} %copy-done.11) | copy-start | bytes 10696
  347.3 31.3 %copy-start.21 = (f32[3]{0:T(128)S(1)}, f32[3]{0:T(128)}, u32[]{:S(2)}) copy-start(f32[3]{0:T(128)} %get-tuple-element.173) | copy-start | bytes 40
  347.6 3.4 collective-permute-start.36
  349.5 5.7 %collective-permute-start.37 = (f32[3,1,9,33]{3,2,1,0:T(8,128)S(1)}, f32[3,1,9,33]{3,2,1,0:T(8,128)S(1)}, u32[]{:S(2)}, u32[]{:S(2)}) collective-permute-start(f32[3,1,9,33]{3,2,1,0:T(8,128)S(1)} %get-tuple-element.129), channel_id=1, source_target_pairs={{1,0},{2,1},{3,2},{5,4},{6,5},{7,6},{9,8},{10,9},{11,10},{13,12},{... | collective-permute-start | bytes 10700 | tf_op jit(solution)/shard_map/ppermute | solution.py:60
  355.3 9.7 %collective-permute-start.38 = (f32[3,3,1,33]{3,2,1,0:T(1,128)S(1)}, f32[3,3,1,33]{3,2,1,0:T(1,128)S(1)}, u32[]{:S(2)}, u32[]{:S(2)}) collective-permute-start(f32[3,3,1,33]{3,2,1,0:T(1,128)S(1)} %pad_maximum_fusion.24), channel_id=1, source_target_pairs={{0,16},{16,32},{32,48},{48,64},{64,80},{80,96},{96,112},{112,128},... | collective-permute-start | bytes 3572 | tf_op jit(solution)/shard_map/ppermute | solution.py:59
  365.0 3.2 collective-permute-start.39
  368.4 3.9 %collective-permute-start.40 = (f32[3,3,9,1]{3,2,1,0:T(8,128)S(1)}, f32[3,3,9,1]{3,2,1,0:T(8,128)S(1)}, u32[]{:S(2)}, u32[]{:S(2)}) collective-permute-start(f32[3,3,9,1]{3,2,1,0:T(8,128)S(1)} %get-tuple-element.123), channel_id=1, source_target_pairs={{0,4},{4,8},{8,12},{1,5},{5,9},{9,13},{2,6},{6,10},{10,14},{3,7},{... | collective-permute-start | bytes 980 | tf_op jit(solution)/shard_map/ppermute | solution.py:59
  370.3 6.2 %collective-permute-start.41 = (f32[3,3,9,1]{3,2,1,0:T(8,128)S(1)}, f32[3,3,9,1]{3,2,1,0:T(8,128)S(1)}, u32[]{:S(2)}, u32[]{:S(2)}) collective-permute-start(f32[3,3,9,1]{3,2,1,0:T(8,128)S(1)} %get-tuple-element.124), channel_id=1, source_target_pairs={{4,0},{8,4},{12,8},{5,1},{9,5},{13,9},{6,2},{10,6},{14,10},{7,3},{... | collective-permute-start | bytes 980 | tf_op jit(solution)/shard_map/ppermute | solution.py:60
  (23 other events, 99.9 us)
